TPU v7x, 512 devices: a whole 4x8x8 slice. The times are simulated.
512 devices in a mesh: rows: 32 (over y, x), vocab: 16 (over z, core).
Axes of the slice: x: 4, y: 8, z: 8, core: 2. Of those that a mesh axis runs over, the one named last changes fastest.
Arguments:
- hidden: bfloat16 [12288, 8192], P('rows', 'vocab'), may hold values from -128 to 128
- head: bfloat16 [8192, 8192], P('rows', 'vocab'), may hold values from -4 to 4
- targets: int32 [12288], P('rows'), may hold values from 0 to 128255
- live: int32 [12288], P('rows'), may hold values from 0 to 1, as said below
- prior_lse: float32 [12288], P('rows'), may hold values from 10 to 18
- prior_mean: float32 [12288], P('rows'), may hold values from 2 to 8
- prior_target: float32 [12288], P('rows'), may hold values from -12 to 12
- seq_lengths: int32 [32], replicated, may hold values from 1 to 768, 12288 in all
Outputs:
- logprob: float32 [12288], P(('rows', 'vocab'))
- entropy: float32 [12288], P(('rows', 'vocab'))
- seq_score: float32 [32], replicated
Inputs may be any that keep to these rules, and one draw needn't show every extreme that they name: Within the 384 rows of each index of rows, the live rows come first; every such index has at least 48 live rows and some index has all 384.
All inputs are finite; a program needn't handle non-finite values.
Results may differ from a plain program's by a relative error of at most 0.0003.
Values may be sent and summed in bfloat16 or wider, within the bound.
No kernel may reach another device: no remote copies, remote signals or barrier semaphores. Data moves between devices by JAX's collectives and lax.ppermute only.
A program may use at most 64 MiB of HBM per device.

v0:
```python
import jax
import jax.numpy as jnp
from jax import lax
from jax.sharding import PartitionSpec as P

VOCAB = 128256
SEQS = 32
GSIZE = 8


def finish_rows(block_peak, block_mass, block_moment, block_target, live, prior_lse, prior_mean):
    highest = jnp.maximum(block_peak, prior_lse)
    earlier = jnp.exp(prior_lse - highest)
    scaled = jnp.exp(block_peak - highest)
    total_mass = earlier + block_mass * scaled
    norm_log = highest + jnp.log(total_mass)
    average = (earlier * prior_mean + scaled * block_moment) / total_mass
    keeping = live.astype(jnp.float32)
    return (keeping * (block_target - norm_log), keeping * (norm_log - average))


def local(hidden, head, targets, live, prior_lse, prior_mean, prior_target, seq_lengths):
    rows_here = hidden.shape[0]
    cols_here = head.shape[1]
    spread = lax.axis_size("vocab")
    which = lax.axis_index("vocab")
    block_first = VOCAB - cols_here * spread
    first_col = block_first + which * cols_here
    gathered = lax.all_gather(hidden, "vocab", axis=1, tiled=True)
    logits = jnp.dot(
        gathered,
        lax.all_gather(head, "rows", axis=0, tiled=True),
        preferred_element_type=jnp.float32,
    )
    row_peak = jnp.max(logits, axis=1)
    weights = jnp.exp(logits - row_peak[:, None])
    row_mass = jnp.sum(weights, axis=1)
    moment = jnp.sum(weights * logits, axis=1)
    column = targets - first_col
    columns = lax.broadcasted_iota(jnp.int32, logits.shape, 1)
    picked = jnp.sum(jnp.where(columns == column[:, None], logits, jnp.zeros_like(logits)), axis=1)
    share = rows_here // spread
    begin = which * share

    def own_rows(values):
        return lax.dynamic_slice_in_dim(values, begin, share, 0)

    highest = lax.pmax(row_peak, "vocab")
    factor = jnp.exp(row_peak - highest)
    mass_all, moment_all, picked_all = lax.psum(
        (row_mass * factor, moment * factor, picked), "vocab"
    )
    peak_share = own_rows(highest)
    mass_share = own_rows(mass_all)
    moment_share = own_rows(moment_all)
    picked_share = own_rows(picked_all)
    target_share = own_rows(targets)
    block_target = jnp.where(target_share >= block_first, picked_share, own_rows(prior_target))
    logprob, entropy = finish_rows(
        peak_share,
        mass_share,
        moment_share,
        block_target,
        own_rows(live),
        own_rows(prior_lse),
        own_rows(prior_mean),
    )
    global_rows = lax.axis_index("rows") * rows_here + begin + jnp.arange(share, dtype=jnp.int32)
    endings = jnp.cumsum(seq_lengths)
    member = jnp.sum((global_rows[:, None] >= endings[None, :]).astype(jnp.int32), axis=1)
    onehot = (member[:, None] == jnp.arange(SEQS, dtype=jnp.int32)[None, :]).astype(jnp.float32)
    partial_sums = jnp.sum(onehot * logprob[:, None], axis=0)
    sums = lax.psum(partial_sums, ("rows", "vocab"))
    seq_mean = sums / seq_lengths.astype(jnp.float32)
    grouped = seq_mean.reshape(SEQS // GSIZE, GSIZE)
    seq_score = (grouped - jnp.mean(grouped, axis=1, keepdims=True)).reshape(SEQS)
    return (logprob, entropy, seq_score)


def solution(mesh):
    return jax.shard_map(
        local,
        mesh=mesh,
        in_specs=(
            P("rows", "vocab"),
            P("rows", "vocab"),
            P("rows"),
            P("rows"),
            P("rows"),
            P("rows"),
            P("rows"),
            P(),
        ),
        out_specs=(P(("rows", "vocab")), P(("rows", "vocab")), P()),
        check_vma=False,
    )
```

profile of v0, /device:TPU:1, one launch (start us, length us, event | category | flops | bytes accessed | tf_op | source)
XLA Modules:
  0.0 332.5 jit_solution(5648980550424565232)
XLA Ops:
  7.2 0.0 all-gather.3.cloned.1.call-start
  7.2 0.7 all-gather.3.cloned.1.call-update
  7.9 0.0 all-gather.5.cloned.1.call-start
  7.9 0.7 all-gather.5.cloned.1.call-update
  8.7 0.7 copy.13
  9.4 0.1 reduce-window.8
  9.4 0.1 reduce
  9.6 0.2 convert_reduce_fusion
  9.8 0.7 broadcast_subtract_fusion
  10.4 0.0 copy-start
  10.4 55.1 %all-gather.3.cloned.1.call-done = bf16[384,8192]{1,0:T(8,128)(2,1)} async-done(((bf16[384,512]{1,0:T(8,128)(2,1)}), bf16[384,8192]{1,0:T(8,128)(2,1)}) %all-gather.3.cloned.1.call-update) | async-done | bytes 6291472 | tf_op jit(solution)/shard_map/all_gather | solution.py:29
  65.6 103.9 %all-gather.5.cloned.1.call-done = bf16[8192,512]{1,0:T(8,128)(2,1)} async-done(((bf16[256,512]{1,0:T(8,128)(2,1)}), bf16[8192,512]{1,0:T(8,128)(2,1)}) %all-gather.5.cloned.1.call-update) | async-done | bytes 8388624 | tf_op jit(solution)/shard_map/all_gather | solution.py:32
  169.4 8.0 %fusion.5 = (f32[384]{0:T(512)S(1)}, f32[384,512]{1,0:T(8,128)S(1)}) fusion(bf16[384,8192]{1,0:T(8,128)(2,1)} %all-gather.3.cloned.1.call-done, bf16[8192,512]{1,0:T(8,128)(2,1)} %all-gather.5.cloned.1.call-done), kind=kOutput, calls=%fused_computation.24 | convolution fusion | flops 3221421568 | bytes 15468032 | tf_op jit(solution)/shard_map/dot_general | solution.py:30
  177.4 25.1 %pmax.7 = f32[384]{0:T(512)S(1)} all-reduce(f32[384]{0:T(512)S(1)} %get-tuple-element.13), channel_id=1, replica_groups=mesh['rows'=32,'vocab'=16] {'vocab'}, use_global_device_ids=true, to_apply=%region_3.4 | all-reduce | flops 384 | bytes 3072 | tf_op jit(solution)/shard_map/pmax | solution.py:48
  202.5 0.5 multiply_reduce_fusion
  203.0 25.8 %all-reduce = (f32[384]{0:T(512)S(1)}, f32[384]{0:T(512)S(1)}, f32[384]{0:T(512)S(1)}) all-reduce(f32[384]{0:T(512)S(1)} %get-tuple-element.5, f32[384]{0:T(512)S(1)} %get-tuple-element.12, f32[384]{0:T(512)S(1)} %get-tuple-element.11), channel_id=1, replica_groups=mesh['rows'=32,'vocab'=16] {'vocab'}, use_global_device_ids=true, to_apply=%region_1.0 | all-reduce | flops 1152 | bytes 9216 | tf_op jit(solution)/shard_map/psum | solution.py:50
  228.9 1.4 subtract_multiply_fusion
  230.2 0.0 copy-start.1
  230.2 0.1 select_reduce_fusion.1
  230.3 94.4 %psum.31 = f32[32]{0:T(128)S(1)} all-reduce(f32[32]{0:T(128)S(1)} %select_reduce_fusion.1), channel_id=1, replica_groups=mesh['rows'=32,'vocab'=16] {'rows','vocab'}, use_global_device_ids=true, to_apply=%region_11.12 | all-reduce | flops 32 | bytes 256 | tf_op jit(solution)/shard_map/psum | solution.py:73
  324.7 0.0 copy-done
  324.7 0.1 reshape.49
  324.8 0.1 reduce_sum.59
  325.0 0.1 sub.49
  325.0 0.1 sub.50
  325.1 0.5 sub.51
  325.6 0.0 copy-done.1
  (4 shorter events, 0.0 us)
Async XLA Ops:
  7.2 58.4 %all-gather.3.cloned.1.call-start = ((), (), s32[]{:S(2)}) async-start(), calls=%async_computation | async-start | bytes 6684672 | tf_op jit(solution)/shard_map/all_gather | solution.py:29
  7.9 161.5 %all-gather.5.cloned.1.call-start = ((), (), s32[]{:S(2)}) async-start(), calls=%async_computation.1 | async-start | bytes 8650752 | tf_op jit(solution)/shard_map/all_gather | solution.py:32
  10.4 314.3 %copy-start = (s32[32]{0:T(128)S(1)}, s32[32]{0:T(128)}, u32[]{:S(2)}) copy-start(s32[32]{0:T(128)} %param.15) | copy-start | bytes 388
  230.2 95.4 %copy-start.1 = (f32[24]{0:T(128)}, f32[24]{0:T(128)S(1)}, u32[]{:S(2)}) copy-start(f32[24]{0:T(128)S(1)} %get-tuple-element.10) | copy-start | bytes 292
Sparse Core Ops, SparseCore 0:
  10.1 55.3 all-gather.2
  68.7 100.6 all-gather.4
where the time goes:
time: 333 us; the launch traced here: 332 us
  waiting for transfers between devices  160 us (48%)
  blocking collectives  145 us (44%)
  between operations  14.1 us (4%)
  matrix products  8 us (2%)
  other arithmetic  3.64 us (1%)
    all_gather x1, waiting for transfers between devices, local(): lax.all_gather(head, 'rows', axis=0, tiled=True)  104 us
    psum x1, blocking collectives, local(): sums = lax.psum(partial_sums, ('rows', 'vocab'))  94.4 us
    all_gather x1, waiting for transfers between devices, local(): gathered = lax.all_gather(hidden, 'vocab', axis=1, tiled=True)  55.1 us
    psum x1, blocking collectives, local(): lax.psum((row_mass * factor, moment * factor, picked), 'vocab')  25.8 us
    pmax x1, blocking collectives, local(): highest = lax.pmax(row_peak, 'vocab')  25.1 us
    dot_general x1, matrix products, local(): jnp.dot(gathered, lax.all_gather(head, 'rows', axis=0, tiled=True), prefe...  8 us
  transfers between devices with their start and end apart: 2, of which 2 were waited for; matrix products, arithmetic and copies ran while one was open for 1% of the time, Pallas kernels for 0%

commit v1 on v0

--- a/solution.py
+++ b/solution.py
@@ -6,6 +6,31 @@
 VOCAB = 128256
 SEQS = 32
 GSIZE = 8
+
+
+def render_cycles(ndim_at, shard_in, mesh_dim):
+    mixed_arr = lax.axis_size(mesh_dim)
+    r2 = lax.axis_index(mesh_dim)
+    b_now, everything, w1 = (mixed_arr, r2, shard_in.shape[ndim_at])
+    fields = [(ix, (ix + 1) % b_now) for ix in range(b_now)]
+    z2 = jnp.zeros(
+        (*shard_in.shape[:ndim_at], b_now * w1, *shard_in.shape[ndim_at + 1 :]), shard_in.dtype
+    )
+    z2 = lax.dynamic_update_slice_in_dim(z2, shard_in, everything * w1, axis=ndim_at)
+    near = now = shard_in
+    y = b_now // 2
+    steps_seen = [(ix, (ix - 1) % b_now) for ix in range(b_now)]
+    for hop_no in range(1, y + 1):
+        near = lax.ppermute(near, mesh_dim, fields)
+        z2 = lax.dynamic_update_slice_in_dim(
+            z2, near, (everything - hop_no) % b_now * w1, axis=ndim_at
+        )
+        if hop_no < b_now - y:
+            now = lax.ppermute(now, mesh_dim, perm=steps_seen)
+            z2 = lax.dynamic_update_slice_in_dim(
+                z2, now, (everything + hop_no) % b_now * w1, axis=ndim_at
+            )
+    return z2
 
 
 def finish_rows(block_peak, block_mass, block_moment, block_target, live, prior_lse, prior_mean):
@@ -26,7 +51,7 @@
     which = lax.axis_index("vocab")
     block_first = VOCAB - cols_here * spread
     first_col = block_first + which * cols_here
-    gathered = lax.all_gather(hidden, "vocab", axis=1, tiled=True)
+    gathered = render_cycles(1, hidden, "vocab")
     logits = jnp.dot(
         gathered,
         lax.all_gather(head, "rows", axis=0, tiled=True),

time: 333 us -> 283 us (0.85)
  waiting for transfers between devices: 160 us -> 48.6 us
  starting transfers between devices: 0.08 us -> 40.5 us
  local copies, waits for them, and re-layouts: 0.99 us -> 19.1 us
    all_gather x1, waiting for transfers between devices: 104 us -> 41.5 us  [local(): lax.all_gather(head, 'rows', axis=0, tiled=True)]
    all_gather x1 -> x0, waiting for transfers between devices: 55.1 us -> none  [local(): gathered = lax.all_gather(hidden, 'vocab', axis=1, tiled=True)]
    ppermute x0 -> x15, starting transfers between devices: none -> 40.5 us  [the longest x7 33.4 us: render_cycles(): now = lax.ppermute(now, mesh_dim, perm=steps_seen)]
    dynamic_update_slice x0 -> x16, local copies, waits for them, and re-layouts: none -> 14.1 us  [the longest x8 7.45 us: render_cycles(): lax.dynamic_update_slice_in_dim(z2, near, (everything - hop_no) % b_now *...]
    ppermute x0 -> x15, waiting for transfers between devices: none -> 6.41 us  [the longest x8 5.45 us: render_cycles(): near = lax.ppermute(near, mesh_dim, fields)]
    broadcast_in_dim x0 -> x1, local copies, waits for them, and re-layouts: none -> 3.46 us  [render_cycles(): jnp.zeros((*shard_in.shape[:ndim_at], b_now * w1, *shard_in.shape[ndim_at...]
  transfers between devices with their start and end apart: 2 -> 16, of which waited for: 2 -> 9; matrix products, arithmetic and copies ran while one was open for 1% -> 8% of each run, Pallas kernels for 0% -> 0%
where the time goes in v1:
time: 283 us
  blocking collectives  145 us (51%)
  waiting for transfers between devices  48.6 us (17%)
  starting transfers between devices  40.5 us (14%)
  local copies, waits for them, and re-layouts  19.1 us (7%)
  between operations  14.4 us (5%)
  matrix products  8 us (3%)
  other arithmetic  6.64 us (2%)
    psum x1, blocking collectives, local(): sums = lax.psum(partial_sums, ('rows', 'vocab'))  94.4 us
    all_gather x1, waiting for transfers between devices, local(): lax.all_gather(head, 'rows', axis=0, tiled=True)  41.5 us
    ppermute x7, starting transfers between devices, render_cycles(): now = lax.ppermute(now, mesh_dim, perm=steps_seen)  33.4 us
    psum x1, blocking collectives, local(): lax.psum((row_mass * factor, moment * factor, picked), 'vocab')  25.8 us
    pmax x1, blocking collectives, local(): highest = lax.pmax(row_peak, 'vocab')  25.1 us
    dot_general x1, matrix products, local(): jnp.dot(gathered, lax.all_gather(head, 'rows', axis=0, tiled=True), prefe...  8 us
    dynamic_update_slice x8, local copies, waits for them, and re-layouts, render_cycles(): lax.dynamic_update_slice_in_dim(z2, near, (everything - hop_no) % b_now *...  7.45 us
    ppermute x8, starting transfers between devices, render_cycles(): near = lax.ppermute(near, mesh_dim, fields)  7.12 us
  transfers between devices with their start and end apart: 16, of which 9 were waited for; matrix products, arithmetic and copies ran while one was open for 8% of the time, Pallas kernels for 0%

profile of v1, /device:TPU:1, one launch (start us, length us, event | category | flops | bytes accessed | tf_op | source)
XLA Modules:
  0.0 282.7 jit_solution(294875742223112869)
XLA Ops:
  7.2 0.0 all-gather.2.cloned.1.call-start
  7.2 0.7 all-gather.2.cloned.1.call-update
  7.9 3.5 %collective-permute-start = (bf16[384,512]{1,0:T(8,128)(2,1)}, bf16[384,512]{1,0:T(8,128)(2,1)S(1)}, u32[]{:S(2)}, u32[]{:S(2)}) collective-permute-start(bf16[384,512]{1,0:T(8,128)(2,1)} %param.8), channel_id=1, source_target_pairs={{0,1},{1,2},{2,3},{3,4},{4,5},{5,6},{6,7},{7,8},{8,9},{9,10},{10,1... | collective-permute-start | bytes 1179656 | tf_op jit(solution)/shard_map/ppermute | solution.py:24
  11.4 3.4 %collective-permute-start.1 = (bf16[384,512]{1,0:T(8,128)(2,1)}, bf16[384,512]{1,0:T(8,128)(2,1)S(1)}, u32[]{:S(2)}, u32[]{:S(2)}) collective-permute-start(bf16[384,512]{1,0:T(8,128)(2,1)} %param.8), channel_id=1, source_target_pairs={{0,15},{1,0},{2,1},{3,2},{4,3},{5,4},{6,5},{7,6},{8,7},{9,8},{10,9... | collective-permute-start | bytes 1179656 | tf_op jit(solution)/shard_map/ppermute | solution.py:29
  14.8 1.6 collective-permute-done
  16.4 2.4 collective-permute-start.2
  18.8 0.3 collective-permute-done.1
  19.1 4.5 %collective-permute-start.3 = (bf16[384,512]{1,0:T(8,128)(2,1)S(1)}, bf16[384,512]{1,0:T(8,128)(2,1)S(1)}, u32[]{:S(2)}, u32[]{:S(2)}) collective-permute-start(bf16[384,512]{1,0:T(8,128)(2,1)S(1)} %collective-permute-done.1), channel_id=1, source_target_pairs={{0,15},{1,0},{2,1},{3,2},{4,3},{5,4},{6,5},{7,6},{8,7},{9,8},{10,9... | collective-permute-start | bytes 1179656 | tf_op jit(solution)/shard_map/ppermute | solution.py:29
  23.6 1.2 collective-permute-done.2
  24.8 1.2 collective-permute-start.4
  26.0 0.3 collective-permute-done.3
  26.3 5.7 %collective-permute-start.5 = (bf16[384,512]{1,0:T(8,128)(2,1)S(1)}, bf16[384,512]{1,0:T(8,128)(2,1)S(1)}, u32[]{:S(2)}, u32[]{:S(2)}) collective-permute-start(bf16[384,512]{1,0:T(8,128)(2,1)S(1)} %collective-permute-done.3), channel_id=1, source_target_pairs={{0,15},{1,0},{2,1},{3,2},{4,3},{5,4},{6,5},{7,6},{8,7},{9,8},{10,9... | collective-permute-start | bytes 1179656 | tf_op jit(solution)/shard_map/ppermute | solution.py:29
  32.0 1.2 collective-permute-done.4
  33.2 0.0 collective-permute-start.6
  33.2 1.3 broadcast_subtract_fusion
  34.5 0.0 collective-permute-done.5
  34.5 7.2 %collective-permute-start.7 = (bf16[384,512]{1,0:T(8,128)(2,1)S(1)}, bf16[384,512]{1,0:T(8,128)(2,1)S(1)}, u32[]{:S(2)}, u32[]{:S(2)}) collective-permute-start(bf16[384,512]{1,0:T(8,128)(2,1)S(1)} %collective-permute-done.5), channel_id=1, source_target_pairs={{0,15},{1,0},{2,1},{3,2},{4,3},{5,4},{6,5},{7,6},{8,7},{9,8},{10,9... | collective-permute-start | bytes 1179656 | tf_op jit(solution)/shard_map/ppermute | solution.py:29
  41.7 0.5 iota_add_fusion
  42.2 1.3 copy.13
  43.5 0.8 reduce-window.8
  44.3 0.6 reduce
  44.9 0.0 collective-permute-done.6
  44.9 0.9 convert_reduce_fusion
  46.1 3.5 %broadcast_in_dim.4 = bf16[384,8192]{1,0:T(8,128)(2,1)} broadcast(bf16[]{:T(256)} %constant.111.clone.1), dimensions={} | broadcast | bytes 6291458 | tf_op jit(solution)/shard_map/broadcast_in_dim | solution.py:16
  49.6 0.9 constant_dynamic-update-slice_fusion.15
  50.4 0.9 constant_dynamic-update-slice_fusion.14
  51.3 0.0 collective-permute-done.7
  51.3 3.8 %collective-permute-start.9 = (bf16[384,512]{1,0:T(8,128)(2,1)S(1)}, bf16[384,512]{1,0:T(8,128)(2,1)S(1)}, u32[]{:S(2)}, u32[]{:S(2)}) collective-permute-start(bf16[384,512]{1,0:T(8,128)(2,1)S(1)} %collective-permute-done.7), channel_id=1, source_target_pairs={{0,15},{1,0},{2,1},{3,2},{4,3},{5,4},{6,5},{7,6},{8,7},{9,8},{10,9... | collective-permute-start | bytes 1179656 | tf_op jit(solution)/shard_map/ppermute | solution.py:29
  55.1 0.8 constant_dynamic-update-slice_fusion.13
  56.0 0.8 constant_dynamic-update-slice_fusion.12
  56.8 0.8 constant_dynamic-update-slice_fusion.11
  57.6 0.8 constant_dynamic-update-slice_fusion.10
  58.4 0.2 collective-permute-done.9
  58.6 4.6 %collective-permute-start.11 = (bf16[384,512]{1,0:T(8,128)(2,1)S(1)}, bf16[384,512]{1,0:T(8,128)(2,1)S(1)}, u32[]{:S(2)}, u32[]{:S(2)}) collective-permute-start(bf16[384,512]{1,0:T(8,128)(2,1)S(1)} %collective-permute-done.9), channel_id=1, source_target_pairs={{0,15},{1,0},{2,1},{3,2},{4,3},{5,4},{6,5},{7,6},{8,7},{9,8},{10,9... | collective-permute-start | bytes 1179656 | tf_op jit(solution)/shard_map/ppermute | solution.py:29
  63.3 0.8 constant_dynamic-update-slice_fusion.9
  64.1 0.0 collective-permute-done.10
  64.1 0.0 collective-permute-start.12
  64.1 0.8 constant_dynamic-update-slice_fusion.8
  64.9 0.8 constant_dynamic-update-slice_fusion.7
  65.7 1.8 constant_dynamic-update-slice_fusion.6
  67.5 4.2 %collective-permute-start.13 = (bf16[384,512]{1,0:T(8,128)(2,1)S(1)}, bf16[384,512]{1,0:T(8,128)(2,1)S(1)}, u32[]{:S(2)}, u32[]{:S(2)}) collective-permute-start(bf16[384,512]{1,0:T(8,128)(2,1)S(1)} %collective-permute-done.11), channel_id=1, source_target_pairs={{0,15},{1,0},{2,1},{3,2},{4,3},{5,4},{6,5},{7,6},{8,7},{9,8},{10,9... | collective-permute-start | bytes 1179656 | tf_op jit(solution)/shard_map/ppermute | solution.py:29
  71.7 0.8 constant_dynamic-update-slice_fusion.5
  72.5 0.0 collective-permute-done.12
  72.5 0.0 collective-permute-start.14
  72.5 0.8 constant_dynamic-update-slice_fusion.4
  73.3 0.8 constant_dynamic-update-slice_fusion.3
  74.1 0.8 constant_dynamic-update-slice_fusion.2
  74.9 0.1 collective-permute-done.13
  75.0 0.8 constant_dynamic-update-slice_fusion.1
  75.8 1.4 collective-permute-done.14
  77.2 0.8 constant_dynamic-update-slice_fusion
  78.0 41.5 %all-gather.2.cloned.1.call-done = bf16[8192,512]{1,0:T(8,128)(2,1)} async-done(((bf16[256,512]{1,0:T(8,128)(2,1)}), bf16[8192,512]{1,0:T(8,128)(2,1)}) %all-gather.2.cloned.1.call-update) | async-done | bytes 8388624 | tf_op jit(solution)/shard_map/all_gather | solution.py:57
  119.6 8.0 %fusion.5 = (f32[384]{0:T(512)S(1)}, f32[384,512]{1,0:T(8,128)S(1)}) fusion(bf16[384,8192]{1,0:T(8,128)(2,1)} %constant_dynamic-update-slice_fusion, bf16[8192,512]{1,0:T(8,128)(2,1)} %all-gather.2.cloned.1.call-done), kind=kOutput, calls=%fused_computation.40 | convolution fusion | flops 3221421568 | bytes 15468032 | tf_op jit(solution)/shard_map/dot_general | solution.py:55
  127.6 25.1 %pmax.7 = f32[384]{0:T(512)S(1)} all-reduce(f32[384]{0:T(512)S(1)} %get-tuple-element.13), channel_id=1, replica_groups=mesh['rows'=32,'vocab'=16] {'vocab'}, use_global_device_ids=true, to_apply=%region_3.4 | all-reduce | flops 384 | bytes 3072 | tf_op jit(solution)/shard_map/pmax | solution.py:73
  152.7 0.5 multiply_reduce_fusion
  153.2 25.8 %all-reduce = (f32[384]{0:T(512)S(1)}, f32[384]{0:T(512)S(1)}, f32[384]{0:T(512)S(1)}) all-reduce(f32[384]{0:T(512)S(1)} %get-tuple-element.5, f32[384]{0:T(512)S(1)} %get-tuple-element.12, f32[384]{0:T(512)S(1)} %get-tuple-element.11), channel_id=1, replica_groups=mesh['rows'=32,'vocab'=16] {'vocab'}, use_global_device_ids=true, to_apply=%region_1.2 | all-reduce | flops 1152 | bytes 9216 | tf_op jit(solution)/shard_map/psum | solution.py:75
  179.0 1.4 subtract_multiply_fusion
  180.4 0.1 select_reduce_fusion.1
  180.5 94.4 %psum.31 = f32[32]{0:T(128)S(1)} all-reduce(f32[32]{0:T(128)S(1)} %select_reduce_fusion.1), channel_id=1, replica_groups=mesh['rows'=32,'vocab'=16] {'rows','vocab'}, use_global_device_ids=true, to_apply=%region_11.12 | all-reduce | flops 32 | bytes 256 | tf_op jit(solution)/shard_map/psum | solution.py:98
  274.9 0.1 reshape.49
  275.0 0.1 reduce_sum.59
  275.1 0.1 sub.81
  275.2 0.1 sub.82
  275.3 0.5 sub.83
  (15 shorter events, 0.0 us)
Async XLA Ops:
  7.2 42.4 %copy-start = (bf16[384,512]{1,0:T(8,128)(2,1)S(1)}, bf16[384,512]{1,0:T(8,128)(2,1)}, u32[]{:S(2)}) copy-start(bf16[384,512]{1,0:T(8,128)(2,1)} %param.8) | copy-start | bytes 1179652
  7.2 112.4 %all-gather.2.cloned.1.call-start = ((), (), s32[]{:S(2)}) async-start(), calls=%async_computation | async-start | bytes 8650752 | tf_op jit(solution)/shard_map/all_gather | solution.py:57
  7.9 8.5 %collective-permute-start = (bf16[384,512]{1,0:T(8,128)(2,1)}, bf16[384,512]{1,0:T(8,128)(2,1)S(1)}, u32[]{:S(2)}, u32[]{:S(2)}) collective-permute-start(bf16[384,512]{1,0:T(8,128)(2,1)} %param.8), channel_id=1, source_target_pairs={{0,1},{1,2},{2,3},{3,4},{4,5},{5,6},{6,7},{7,8},{8,9},{9,10},{10,1... | collective-permute-start | bytes 1179656 | tf_op jit(solution)/shard_map/ppermute | solution.py:24
  11.4 7.7 %collective-permute-start.1 = (bf16[384,512]{1,0:T(8,128)(2,1)}, bf16[384,512]{1,0:T(8,128)(2,1)S(1)}, u32[]{:S(2)}, u32[]{:S(2)}) collective-permute-start(bf16[384,512]{1,0:T(8,128)(2,1)} %param.8), channel_id=1, source_target_pairs={{0,15},{1,0},{2,1},{3,2},{4,3},{5,4},{6,5},{7,6},{8,7},{9,8},{10,9... | collective-permute-start | bytes 1179656 | tf_op jit(solution)/shard_map/ppermute | solution.py:29
  16.4 8.4 %collective-permute-start.2 = (bf16[384,512]{1,0:T(8,128)(2,1)S(1)}, bf16[384,512]{1,0:T(8,128)(2,1)S(1)}, u32[]{:S(2)}, u32[]{:S(2)}) collective-permute-start(bf16[384,512]{1,0:T(8,128)(2,1)S(1)} %collective-permute-done), channel_id=1, source_target_pairs={{0,1},{1,2},{2,3},{3,4},{4,5},{5,6},{6,7},{7,8},{8,9},{9,10},{10,1... | collective-permute-start | bytes 1179656 | tf_op jit(solution)/shard_map/ppermute | solution.py:24
  19.1 7.2 %collective-permute-start.3 = (bf16[384,512]{1,0:T(8,128)(2,1)S(1)}, bf16[384,512]{1,0:T(8,128)(2,1)S(1)}, u32[]{:S(2)}, u32[]{:S(2)}) collective-permute-start(bf16[384,512]{1,0:T(8,128)(2,1)S(1)} %collective-permute-done.1), channel_id=1, source_target_pairs={{0,15},{1,0},{2,1},{3,2},{4,3},{5,4},{6,5},{7,6},{8,7},{9,8},{10,9... | collective-permute-start | bytes 1179656 | tf_op jit(solution)/shard_map/ppermute | solution.py:29
  24.8 8.4 %collective-permute-start.4 = (bf16[384,512]{1,0:T(8,128)(2,1)S(1)}, bf16[384,512]{1,0:T(8,128)(2,1)S(1)}, u32[]{:S(2)}, u32[]{:S(2)}) collective-permute-start(bf16[384,512]{1,0:T(8,128)(2,1)S(1)} %collective-permute-done.2), channel_id=1, source_target_pairs={{0,1},{1,2},{2,3},{3,4},{4,5},{5,6},{6,7},{7,8},{8,9},{9,10},{10,1... | collective-permute-start | bytes 1179656 | tf_op jit(solution)/shard_map/ppermute | solution.py:24
  26.3 8.2 %collective-permute-start.5 = (bf16[384,512]{1,0:T(8,128)(2,1)S(1)}, bf16[384,512]{1,0:T(8,128)(2,1)S(1)}, u32[]{:S(2)}, u32[]{:S(2)}) collective-permute-start(bf16[384,512]{1,0:T(8,128)(2,1)S(1)} %collective-permute-done.3), channel_id=1, source_target_pairs={{0,15},{1,0},{2,1},{3,2},{4,3},{5,4},{6,5},{7,6},{8,7},{9,8},{10,9... | collective-permute-start | bytes 1179656 | tf_op jit(solution)/shard_map/ppermute | solution.py:29
  33.2 11.7 %collective-permute-start.6 = (bf16[384,512]{1,0:T(8,128)(2,1)S(1)}, bf16[384,512]{1,0:T(8,128)(2,1)S(1)}, u32[]{:S(2)}, u32[]{:S(2)}) collective-permute-start(bf16[384,512]{1,0:T(8,128)(2,1)S(1)} %collective-permute-done.4), channel_id=1, source_target_pairs={{0,1},{1,2},{2,3},{3,4},{4,5},{5,6},{6,7},{7,8},{8,9},{9,10},{10,1... | collective-permute-start | bytes 1179656 | tf_op jit(solution)/shard_map/ppermute | solution.py:24
  34.5 16.8 %collective-permute-start.7 = (bf16[384,512]{1,0:T(8,128)(2,1)S(1)}, bf16[384,512]{1,0:T(8,128)(2,1)S(1)}, u32[]{:S(2)}, u32[]{:S(2)}) collective-permute-start(bf16[384,512]{1,0:T(8,128)(2,1)S(1)} %collective-permute-done.5), channel_id=1, source_target_pairs={{0,15},{1,0},{2,1},{3,2},{4,3},{5,4},{6,5},{7,6},{8,7},{9,8},{10,9... | collective-permute-start | bytes 1179656 | tf_op jit(solution)/shard_map/ppermute | solution.py:29
  44.9 11.0 %collective-permute-start.8 = (bf16[384,512]{1,0:T(8,128)(2,1)S(1)}, bf16[384,512]{1,0:T(8,128)(2,1)}, u32[]{:S(2)}, u32[]{:S(2)}) collective-permute-start(bf16[384,512]{1,0:T(8,128)(2,1)S(1)} %collective-permute-done.6), channel_id=1, source_target_pairs={{0,1},{1,2},{2,3},{3,4},{4,5},{5,6},{6,7},{7,8},{8,9},{9,10},{10,1... | collective-permute-start | bytes 1179656 | tf_op jit(solution)/shard_map/ppermute | solution.py:24
  51.3 7.3 %collective-permute-start.9 = (bf16[384,512]{1,0:T(8,128)(2,1)S(1)}, bf16[384,512]{1,0:T(8,128)(2,1)S(1)}, u32[]{:S(2)}, u32[]{:S(2)}) collective-permute-start(bf16[384,512]{1,0:T(8,128)(2,1)S(1)} %collective-permute-done.7), channel_id=1, source_target_pairs={{0,15},{1,0},{2,1},{3,2},{4,3},{5,4},{6,5},{7,6},{8,7},{9,8},{10,9... | collective-permute-start | bytes 1179656 | tf_op jit(solution)/shard_map/ppermute | solution.py:29
  56.0 8.1 %collective-permute-start.10 = (bf16[384,512]{1,0:T(8,128)(2,1)}, bf16[384,512]{1,0:T(8,128)(2,1)S(1)}, u32[]{:S(2)}, u32[]{:S(2)}) collective-permute-start(bf16[384,512]{1,0:T(8,128)(2,1)} %collective-permute-done.8), channel_id=1, source_target_pairs={{0,1},{1,2},{2,3},{3,4},{4,5},{5,6},{6,7},{7,8},{8,9},{9,10},{10,1... | collective-permute-start | bytes 1179656 | tf_op jit(solution)/shard_map/ppermute | solution.py:24
  58.6 8.9 %collective-permute-start.11 = (bf16[384,512]{1,0:T(8,128)(2,1)S(1)}, bf16[384,512]{1,0:T(8,128)(2,1)S(1)}, u32[]{:S(2)}, u32[]{:S(2)}) collective-permute-start(bf16[384,512]{1,0:T(8,128)(2,1)S(1)} %collective-permute-done.9), channel_id=1, source_target_pairs={{0,15},{1,0},{2,1},{3,2},{4,3},{5,4},{6,5},{7,6},{8,7},{9,8},{10,9... | collective-permute-start | bytes 1179656 | tf_op jit(solution)/shard_map/ppermute | solution.py:29
  64.1 8.4 %collective-permute-start.12 = (bf16[384,512]{1,0:T(8,128)(2,1)S(1)}, bf16[384,512]{1,0:T(8,128)(2,1)S(1)}, u32[]{:S(2)}, u32[]{:S(2)}) collective-permute-start(bf16[384,512]{1,0:T(8,128)(2,1)S(1)} %collective-permute-done.10), channel_id=1, source_target_pairs={{0,1},{1,2},{2,3},{3,4},{4,5},{5,6},{6,7},{7,8},{8,9},{9,10},{10,1... | collective-permute-start | bytes 1179656 | tf_op jit(solution)/shard_map/ppermute | solution.py:24
  67.5 7.5 %collective-permute-start.13 = (bf16[384,512]{1,0:T(8,128)(2,1)S(1)}, bf16[384,512]{1,0:T(8,128)(2,1)S(1)}, u32[]{:S(2)}, u32[]{:S(2)}) collective-permute-start(bf16[384,512]{1,0:T(8,128)(2,1)S(1)} %collective-permute-done.11), channel_id=1, source_target_pairs={{0,15},{1,0},{2,1},{3,2},{4,3},{5,4},{6,5},{7,6},{8,7},{9,8},{10,9... | collective-permute-start | bytes 1179656 | tf_op jit(solution)/shard_map/ppermute | solution.py:29
  72.5 4.7 %collective-permute-start.14 = (bf16[384,512]{1,0:T(8,128)(2,1)S(1)}, bf16[384,512]{1,0:T(8,128)(2,1)S(1)}, u32[]{:S(2)}, u32[]{:S(2)}) collective-permute-start(bf16[384,512]{1,0:T(8,128)(2,1)S(1)} %collective-permute-done.12), channel_id=1, source_target_pairs={{0,1},{1,2},{2,3},{3,4},{4,5},{5,6},{6,7},{7,8},{8,9},{9,10},{10,1... | collective-permute-start | bytes 1179656 | tf_op jit(solution)/shard_map/ppermute | solution.py:24
  78.0 74.7 %copy-start.1 = (s32[384]{0:T(512)S(1)}, s32[384]{0:T(512)}, u32[]{:S(2)}) copy-start(s32[384]{0:T(512)} %broadcast_subtract_fusion) | copy-start | bytes 4612
  78.0 196.9 %copy-start.2 = (s32[32]{0:T(128)S(1)}, s32[32]{0:T(128)}, u32[]{:S(2)}) copy-start(s32[32]{0:T(128)} %param.15) | copy-start | bytes 388
  180.4 95.4 %copy-start.3 = (f32[24]{0:T(128)}, f32[24]{0:T(128)S(1)}, u32[]{:S(2)}) copy-start(f32[24]{0:T(128)S(1)} %get-tuple-element.10) | copy-start | bytes 292
Sparse Core Ops, SparseCore 0:
  11.2 108.3 all-gather.1
